TPU v7x, 32 devices: a whole 2x2x4 slice. The times are simulated.
32 devices in a mesh: groups: 2 (over y), gx: 4 (over z), gy: 2 (over x), gz: 2 (over core).
Axes of the slice: x: 2, y: 2, z: 4, core: 2. Of those that a mesh axis runs over, the one named last changes fastest.
Arguments:
- parent: bfloat16 [160, 32, 1024], P('groups', 'gx', ('gy', 'gz')), parts along dimension 0, may hold values from -6 to 6
- nest: bfloat16 [160, 24, 1536], P('groups', 'gx', ('gy', 'gz')), parts along dimension 0, may hold values from -6 to 6
- nu_parent: float32 [80], replicated, may hold values from 0.03 to 0.24
- nu_nest: float32 [80], replicated, may hold values from 0.03 to 0.24
- relax: float32 [80], replicated, may hold values from 0.1 to 0.5
- feedback: float32 [80], replicated, may hold values from 0.3 to 1
- vert_mix: float32 [80, 80], replicated, may hold values from -1 to 1
- fp_owner: int32 [4, 4, 256, 1], P('gx', ('gy', 'gz')), may hold values from 0 to 3; in each aligned block of 256 rows (0 to 255, 256 to 511, ..., all dimensions but the last counted through in order) at most 256 rows name the same one
- fp_cell: int32 [4, 4, 256], P('gx', ('gy', 'gz')), may hold values from 0 to 2047
- nest_of: int32 [24], replicated, may hold values from 0 to 2, as said below
Outputs:
- parent_out: bfloat16 [160, 32, 1024], P('groups', 'gx', ('gy', 'gz')), parts along dimension 0
- nest_out: bfloat16 [160, 24, 1536], P('groups', 'gx', ('gy', 'gz')), parts along dimension 0
There are 2 independent parts, one for each index of `groups`. A program takes and returns all parts, laid end to end along the dimension named above; an argument that names none is the same for every part. Nothing has to cross between parts.
Inputs may be any that keep to these rules, and one draw needn't show every extreme that they name: `fp_owner`: within the 256 blocks of one nest tile no parent tile is named more than 256 times; in some nest tiles one is named exactly 256 times. `nest_of`: never falls along the rows; every nest holds one or more rows; nest 1 holds rows 11 and 12.
All inputs are finite; a program needn't handle non-finite values.
Results may differ from a plain program's by a relative error of at most 0.0033.
Values may be sent and summed in bfloat16 or wider, within the bound.
No kernel may reach another device: no remote copies, remote signals or barrier semaphores. Data moves between devices by JAX's collectives and lax.ppermute only.
A program may use at most 64 MiB of HBM per device.

v0:
```python
import jax
import jax.numpy as jnp
from jax import lax
from jax.sharding import PartitionSpec as P

Y_AXES = ("gy", "gz")
HI = lax.Precision.HIGHEST


def shift_pairs(count):
    forward = [(i, i + 1) for i in range(count - 1)]
    backward = [(i + 1, i) for i in range(count - 1)]
    return (forward, backward)


def exchange(blocks):
    fwd_x, bwd_x = shift_pairs(lax.axis_size("gx"))
    fwd_y, bwd_y = shift_pairs(lax.axis_size(Y_AXES))
    last_rows = jnp.concatenate([b[:, -1, :] for b in blocks], axis=1)
    first_rows = jnp.concatenate([b[:, 0, :] for b in blocks], axis=1)
    last_cols = jnp.concatenate([b[:, :, -1] for b in blocks], axis=1)
    first_cols = jnp.concatenate([b[:, :, 0] for b in blocks], axis=1)
    above = lax.ppermute(last_rows, "gx", fwd_x)
    below = lax.ppermute(first_rows, "gx", bwd_x)
    left = lax.ppermute(last_cols, Y_AXES, fwd_y)
    right = lax.ppermute(first_cols, Y_AXES, bwd_y)
    out = []
    xo = 0
    yo = 0
    for b in blocks:
        w, h = (b.shape[2], b.shape[1])
        out.append(
            (
                above[:, xo : xo + w],
                below[:, xo : xo + w],
                left[:, yo : yo + h],
                right[:, yo : yo + h],
            )
        )
        xo += w
        yo += h
    return out


def per_row(values, rows, cols):
    if values.ndim == 1:
        return jnp.broadcast_to(values[:, None], (rows, cols)).reshape(rows * cols)
    return jnp.broadcast_to(values[:, :, None], values.shape + (cols,)).reshape(
        values.shape[0], rows * cols
    )


def flat_stencil(flat, rows, cols, halo, up_w=None, down_w=None):
    above, below, left, right = (h.astype(flat.dtype) for h in halo)
    levels = flat.shape[0]
    up = jnp.concatenate([above, flat[:, :-cols]], axis=1)
    down = jnp.concatenate([flat[:, cols:], below], axis=1)
    col = lax.broadcasted_iota(jnp.int32, (1, rows * cols), 1) % cols
    zero = jnp.zeros((levels, 1), flat.dtype)
    west = jnp.where(
        col == 0, per_row(left, rows, cols), jnp.concatenate([zero, flat[:, :-1]], axis=1)
    )
    east = jnp.where(
        col == cols - 1, per_row(right, rows, cols), jnp.concatenate([flat[:, 1:], zero], axis=1)
    )
    if down_w is not None:
        down = down * down_w[None, :]
        up = up * up_w[None, :]
    return down + up + east + west - 4.0 * flat


def mix_levels(matrix, flat):
    return jnp.dot(matrix, flat, precision=HI, preferred_element_type=jnp.float32)


def nest_segments(nest_of, first, count):
    index_rows = first + jnp.arange(count, dtype=jnp.int32)
    inside = (index_rows >= 0) & (index_rows < nest_of.shape[0])
    return jnp.where(inside, nest_of[jnp.clip(index_rows, 0, nest_of.shape[0] - 1)], -1)


def row_weights(segments):
    left_w = (segments[:-2] == segments[1:-1]).astype(jnp.float32)
    right_w = (segments[2:] == segments[1:-1]).astype(jnp.float32)
    return (left_w, right_w)


def block_expansion(block_rows, block_cols, rows, cols, zero):
    r = lax.broadcasted_iota(jnp.int32, (block_rows * block_cols, rows * cols), 0) + zero
    p = lax.broadcasted_iota(jnp.int32, (block_rows * block_cols, rows * cols), 1)
    hit = (p // cols // 3 == r // block_cols) & (p % cols // 3 == r % block_cols)
    return hit.astype(jnp.float32)


def body(parent, nest, nu_parent, nu_nest, relax, feedback, vert_mix, fp_owner, fp_cell, nest_of):
    levels, p_rows, p_cols = parent.shape
    _, n_rows, n_cols = nest.shape
    tiles_x = lax.axis_size("gx")
    here_x = lax.axis_index("gx")
    zero = jnp.minimum(here_x, 0)
    parent_halo, nest_halo = exchange([parent, nest])
    centre = parent.astype(jnp.float32).reshape(levels, p_rows * p_cols)
    stencil = flat_stencil(centre, p_rows, p_cols, parent_halo)
    flat_parent = mix_levels(vert_mix, centre + nu_parent[:, None] * stencil)
    owners = fp_owner.reshape(-1)
    cells = fp_cell.reshape(-1)
    requests = owners.shape[0]
    slots = 4 * requests // tiles_x
    owner_ids = jnp.arange(tiles_x, dtype=jnp.int32)
    if slots >= requests:
        chosen = owners[None, :] == owner_ids[:, None]
        wanted = jnp.where(chosen, cells[None, :], 0)
        wanted = jnp.pad(wanted, ((0, 0), (0, slots - requests))).reshape(-1)
    else:
        onehot = (owners[:, None] == owner_ids[None, :]).astype(jnp.int32)
        before = jnp.cumsum(onehot, axis=0) - onehot
        order_in = jnp.sum(before * onehot, axis=1)
        places = owners * slots + order_in
        wanted = jnp.zeros((tiles_x * slots,), jnp.int32).at[places].set(cells)
    served_ids = lax.all_to_all(wanted, "gx", split_axis=0, concat_axis=0, tiled=True)
    answers = lax.all_to_all(
        jnp.take(flat_parent, served_ids, axis=1), "gx", split_axis=1, concat_axis=1, tiled=True
    )
    if slots >= requests:
        answers = answers.reshape(levels, tiles_x, slots)[:, :, :requests]
        forcing_flat = answers[:, 0, :]
        for o in range(1, tiles_x):
            forcing_flat = jnp.where(chosen[o][None, :], answers[:, o, :], forcing_flat)
    else:
        forcing_flat = jnp.take(answers, places, axis=1)
    block_rows = n_rows // 3
    block_cols = n_cols // 3
    expand = block_expansion(block_rows, block_cols, n_rows, n_cols, zero)
    forcing_full = jnp.dot(forcing_flat, expand, precision=HI, preferred_element_type=jnp.float32)
    row_start = here_x * n_rows
    left_w, right_w = row_weights(nest_segments(nest_of, row_start - 1, n_rows + 2))
    up_w = per_row(left_w, n_rows, n_cols)
    down_w = per_row(right_w, n_rows, n_cols)
    nest_state = nest.astype(jnp.float32).reshape(levels, n_rows * n_cols)
    halo = nest_halo
    for turn_no in range(3):
        if turn_no > 0:
            shaped = nest_state.astype(jnp.bfloat16).reshape(levels, n_rows, n_cols)
            (halo,) = exchange([shaped])
        stencil_sum = flat_stencil(nest_state, n_rows, n_cols, halo, up_w, down_w)
        moved = nest_state + nu_nest[:, None] * stencil_sum
        moved = moved + relax[:, None] * (forcing_full - moved)
        nest_state = mix_levels(vert_mix, moved)
    block_sum = lax.dot_general(
        nest_state,
        expand,
        (((1,), (1,)), ((), ())),
        precision=HI,
        preferred_element_type=jnp.float32,
    )
    nudge_gap = block_sum / 9.0 - forcing_flat
    if slots >= requests:
        outgoing = jnp.where(chosen[None, :, :], nudge_gap[:, None, :], 0.0)
        outgoing = jnp.pad(outgoing, ((0, 0), (0, 0), (0, slots - requests)))
        outgoing = outgoing.reshape(levels, tiles_x * slots)
    else:
        outgoing = jnp.zeros((levels, tiles_x * slots), jnp.float32).at[:, places].set(nudge_gap)
    incoming = lax.all_to_all(outgoing, "gx", split_axis=1, concat_axis=1, tiled=True)
    summed = jnp.zeros_like(flat_parent).at[:, served_ids].add(incoming)
    parent_out = (flat_parent + feedback[:, None] * summed).astype(jnp.bfloat16)
    return (
        parent_out.reshape(levels, p_rows, p_cols),
        nest_state.astype(jnp.bfloat16).reshape(levels, n_rows, n_cols),
    )


def solution(mesh):
    placed = (
        P("groups", "gx", Y_AXES),
        P("groups", "gx", Y_AXES),
        P(),
        P(),
        P(),
        P(),
        P(),
        P("gx", Y_AXES, None, None),
        P("gx", Y_AXES, None),
        P(),
    )
    return jax.shard_map(
        body,
        mesh=mesh,
        in_specs=placed,
        out_specs=(P("groups", "gx", Y_AXES), P("groups", "gx", Y_AXES)),
        check_vma=False,
    )
```

profile of v0, /device:TPU:1, one launch (start us, length us, event | category | flops | bytes accessed | tf_op | source)
XLA Modules:
  0.0 121.2 jit_solution(3893287503478127455)
XLA Ops:
  3.5 1.4 %collective-permute-start = (bf16[80,640]{1,0:T(8,128)(2,1)}, bf16[80,640]{1,0:T(8,128)(2,1)}, u32[]{:S(2)}, u32[]{:S(2)}) collective-permute-start(bf16[80,640]{1,0:T(8,128)(2,1)} %pad_maximum_fusion), channel_id=1, source_target_pairs={{4,0},{8,4},{12,8},{5,1},{9,5},{13,9},{6,2},{10,6},{14,10},{7,3},{... | collective-permute-start | bytes 307208 | tf_op jit(solution)/shard_map/ppermute | solution.py:24
  5.6 5.3 %collective-permute-start.1 = (bf16[80,640]{1,0:T(8,128)(2,1)}, bf16[80,640]{1,0:T(8,128)(2,1)}, u32[]{:S(2)}, u32[]{:S(2)}) collective-permute-start(bf16[80,640]{1,0:T(8,128)(2,1)} %pad_maximum_fusion.1), channel_id=1, source_target_pairs={{0,4},{4,8},{8,12},{1,5},{5,9},{9,13},{2,6},{6,10},{10,14},{3,7},{... | collective-permute-start | bytes 307208 | tf_op jit(solution)/shard_map/ppermute | solution.py:23
  11.4 4.4 %collective-permute-start.3 = (bf16[80,14]{0,1:T(8,128)(2,1)S(1)}, bf16[80,14]{0,1:T(8,128)(2,1)S(1)}, u32[]{:S(2)}, u32[]{:S(2)}) collective-permute-start(bf16[80,14]{0,1:T(8,128)(2,1)S(1)} %pad_maximum_fusion.3), channel_id=1, source_target_pairs={{0,1},{1,2},{2,3},{4,5},{5,6},{6,7},{8,9},{9,10},{10,11},{12,13},{... | collective-permute-start | bytes 6728 | tf_op jit(solution)/shard_map/ppermute | solution.py:25
  16.1 1.9 %collective-permute-start.2 = (bf16[80,14]{0,1:T(8,128)(2,1)S(1)}, bf16[80,14]{0,1:T(8,128)(2,1)S(1)}, u32[]{:S(2)}, u32[]{:S(2)}) collective-permute-start(bf16[80,14]{0,1:T(8,128)(2,1)S(1)} %pad_maximum_fusion.2), channel_id=1, source_target_pairs={{1,0},{2,1},{3,2},{5,4},{6,5},{7,6},{9,8},{10,9},{11,10},{13,12},{... | collective-permute-start | bytes 6728 | tf_op jit(solution)/shard_map/ppermute | solution.py:26
  18.7 3.6 %all-to-all-start = ((s32[4,256,1]{1,2,0:T(1,128)}), s32[4,256,1]{1,2,0:T(1,128)S(1)}, u32[]{:S(2)}, u32[]{:S(2)}) async-start(s32[4,256,1]{1,2,0:T(1,128)} %compare_select_fusion.1), calls=%async_computation | async-start | bytes 8192 | tf_op jit(solution)/shard_map/all_to_all | solution.py:120
  25.0 1.4 %fusion.134 = (f32[80,2303]{1,0:T(8,128)}, f32[80,2303]{1,0:T(8,128)}) fusion(f32[80,2304]{1,0:T(8,128)S(1)} %bitcast.111), kind=kLoop, calls=%fused_computation.210 | loop fusion | bytes 2947840 | tf_op jit(solution)/shard_map/slice | solution.py:64
  27.2 2.2 %fusion.6 = pred[256,2304]{1,0:T(32,128)(4,1)} fusion(s32[256]{0:T(256)S(1)} %get-tuple-element.58, s32[256]{0:T(256)S(1)} %get-tuple-element.59, s32[2304]{0:T(1024)S(1)} %get-tuple-element.62, s32[2304]{0:T(1024)S(1)} %get-tuple-element.63, s32[256]{0:T(256)S(1)} %get-tuple-element.57, s32[256]{0:T(256)S(1)} %get-tuple-element.60, ...), kind=kLoop, calls=%fused_computation.20 | loop fusion | flops 13565952 | bytes 635904 | tf_op jit(solution)/shard_map/and | solution.py:91
  33.8 2.8 %convolution_bitcast_fusion.2 = f32[80,2048]{1,0:T(8,128)S(1)} fusion(f32[80,80]{1,0:T(8,128)S(1)} %copy-done, f32[80,2048]{1,0:T(8,128)S(1)} %bitcast.115, f32[80,256]{1,0:T(8,128)S(1)} %slice_convert_fusion.3, f32[80,1792]{1,0:T(8,128)} %get-tuple-element.28, f32[80,1792]{1,0:T(8,128)} %get-tuple-element.27, f32[80,256]{1,0:T(8,128)S(1)} %slice_convert_fusion.2, ...), kind=kOutput, calls=%fused_computation.13 | convolution fusion | flops 159088640 | bytes 5272256 | tf_op jit(solution)/shard_map/dot_general | solution.py:73
  36.9 2.8 %gather_fusion.1 = f32[1024,80]{1,0:T(8,128)S(1)} fusion(f32[80,2048]{0,1:T(8,128)S(1)} %copy.93, s32[1024]{0:T(1024)S(1)} %broadcast_clamp_fusion), kind=kCustom, calls=%fused_computation.1 | custom fusion | bytes 659456 | tf_op jit(solution)/shard_map/jit(_take)/gather | solution.py:122
  40.7 4.5 %all-to-all-start.1 = ((f32[80,4,256]{2,0,1:T(8,128)}), f32[80,4,256]{2,0,1:T(8,128)S(1)}, u32[]{:S(2)}, u32[]{:S(2)}) async-start(f32[80,4,256]{2,0,1:T(8,128)} %broadcast_select_fusion.1), calls=%async_computation.1 | async-start | bytes 655360 | tf_op jit(solution)/shard_map/all_to_all | solution.py:121
  47.8 1.5 %slice_convert_fusion = f32[80,384]{1,0:T(8,128)} fusion(bf16[80,640]{1,0:T(8,128)(2,1)} %collective-permute-done.1), kind=kLoop, calls=%fused_computation.131 | loop fusion | flops 30720 | bytes 184320 | tf_op jit(solution)/shard_map/convert_element_type | solution.py:54
  49.3 1.6 %slice_convert_fusion.1 = f32[80,384]{1,0:T(8,128)} fusion(bf16[80,640]{1,0:T(8,128)(2,1)} %collective-permute-done), kind=kLoop, calls=%fused_computation.132 | loop fusion | flops 30720 | bytes 184320 | tf_op jit(solution)/shard_map/convert_element_type | solution.py:54
  50.8 3.9 %all-to-all-done.1 = f32[80,4,256]{2,0,1:T(8,128)S(1)} async-done(((f32[80,4,256]{2,0,1:T(8,128)}), f32[80,4,256]{2,0,1:T(8,128)S(1)}, u32[]{:S(2)}, u32[]{:S(2)}) %all-to-all-start.1) | async-done | bytes 327712 | tf_op jit(solution)/shard_map/all_to_all | solution.py:121
  55.7 3.3 %fusion.145 = (bf16[80,2304]{1,0:T(8,128)(2,1)S(1)}, f32[80,2304]{1,0:T(8,128)S(1)}) fusion(f32[80,80]{1,0:T(8,128)S(1)} %copy-done, f32[80,2304]{1,0:T(8,128)S(1)} %fusion.148, f32[80,2304]{1,0:T(8,128)S(1)} %bitcast.112, f32[80,1920]{1,0:T(8,128)} %get-tuple-element.23, f32[80,384]{1,0:T(8,128)S(1)} %copy-done.16, f32[80,384]{1,0:T(8,128)S(1)} %copy-done.17, ...), kind=kOutput, calls=%fused_computation.221 | convolution fusion | flops 180080640 | bytes 7052800 | tf_op jit(solution)/shard_map/dot_general | solution.py:73
  62.5 4.4 %collective-permute-start.7 = (bf16[80,6]{0,1:T(8,128)(2,1)S(1)}, bf16[80,6]{0,1:T(8,128)(2,1)S(1)}, u32[]{:S(2)}, u32[]{:S(2)}) collective-permute-start(bf16[80,6]{0,1:T(8,128)(2,1)S(1)} %bitcast.154), channel_id=1, source_target_pairs={{0,1},{1,2},{2,3},{4,5},{5,6},{6,7},{8,9},{9,10},{10,11},{12,13},{... | collective-permute-start | bytes 2888 | tf_op jit(solution)/shard_map/ppermute | solution.py:25
  68.2 1.9 %collective-permute-start.6 = (bf16[80,6]{0,1:T(8,128)(2,1)S(1)}, bf16[80,6]{0,1:T(8,128)(2,1)S(1)}, u32[]{:S(2)}, u32[]{:S(2)}) collective-permute-start(bf16[80,6]{0,1:T(8,128)(2,1)S(1)} %bitcast.156), channel_id=1, source_target_pairs={{1,0},{2,1},{3,2},{5,4},{6,5},{7,6},{9,8},{10,9},{11,10},{13,12},{... | collective-permute-start | bytes 2888 | tf_op jit(solution)/shard_map/ppermute | solution.py:26
  77.0 4.9 %collective-permute-start.9 = (bf16[80,384]{1,0:T(8,128)(2,1)S(1)}, bf16[80,384]{1,0:T(8,128)(2,1)}, u32[]{:S(2)}, u32[]{:S(2)}) collective-permute-start(bf16[80,384]{1,0:T(8,128)(2,1)S(1)} %bitcast.143), channel_id=1, source_target_pairs={{0,4},{4,8},{8,12},{1,5},{5,9},{9,13},{2,6},{6,10},{10,14},{3,7},{... | collective-permute-start | bytes 184328 | tf_op jit(solution)/shard_map/ppermute | solution.py:23
  82.5 1.5 %collective-permute-start.8 = (bf16[80,384]{1,0:T(8,128)(2,1)}, bf16[80,384]{1,0:T(8,128)(2,1)}, u32[]{:S(2)}, u32[]{:S(2)}) collective-permute-start(bf16[80,384]{1,0:T(8,128)(2,1)} %bitcast.105), channel_id=1, source_target_pairs={{4,0},{8,4},{12,8},{5,1},{9,5},{13,9},{6,2},{10,6},{14,10},{7,3},{... | collective-permute-start | bytes 184328 | tf_op jit(solution)/shard_map/ppermute | solution.py:24
  84.2 3.3 %collective-permute-start.11 = (bf16[80,6]{0,1:T(8,128)(2,1)S(1)}, bf16[80,6]{0,1:T(8,128)(2,1)S(1)}, u32[]{:S(2)}, u32[]{:S(2)}) collective-permute-start(bf16[80,6]{0,1:T(8,128)(2,1)S(1)} %bitcast.155), channel_id=1, source_target_pairs={{0,1},{1,2},{2,3},{4,5},{5,6},{6,7},{8,9},{9,10},{10,11},{12,13},{... | collective-permute-start | bytes 2888 | tf_op jit(solution)/shard_map/ppermute | solution.py:25
  87.9 1.9 %collective-permute-start.10 = (bf16[80,6]{0,1:T(8,128)(2,1)S(1)}, bf16[80,6]{0,1:T(8,128)(2,1)S(1)}, u32[]{:S(2)}, u32[]{:S(2)}) collective-permute-start(bf16[80,6]{0,1:T(8,128)(2,1)S(1)} %bitcast.157), channel_id=1, source_target_pairs={{1,0},{2,1},{3,2},{5,4},{6,5},{7,6},{9,8},{10,9},{11,10},{13,12},{... | collective-permute-start | bytes 2888 | tf_op jit(solution)/shard_map/ppermute | solution.py:26
  95.1 1.3 %fusion.147 = (bf16[2304,80]{0,1:T(8,128)(2,1)S(1)}, f32[2304,80]{0,1:T(8,128)S(1)}) fusion(f32[80,80]{1,0:T(8,128)S(1)} %copy-done, f32[80,2304]{1,0:T(8,128)S(1)} %fusion.148, f32[80,2304]{1,0:T(8,128)S(1)} %get-tuple-element.50, f32[80,1920]{1,0:T(8,128)S(1)} %copy-done.10, f32[80,384]{1,0:T(8,128)S(1)} %convert_element_type.89, ...), kind=kOutput, calls=%fused_computation.223 | convolution fusion | flops 180080640 | bytes 7052800 | tf_op jit(solution)/shard_map/dot_general | solution.py:73
  98.5 4.7 %all-to-all-start.2 = ((f32[80,4,256]{2,0,1:T(8,128)}), f32[80,4,256]{2,0,1:T(8,128)S(1)}, u32[]{:S(2)}, u32[]{:S(2)}) async-start(f32[80,4,256]{2,0,1:T(8,128)} %broadcast_select_fusion), calls=%async_computation.2 | async-start | bytes 655360 | tf_op jit(solution)/shard_map/all_to_all | solution.py:163
  103.9 8.7 %all-to-all-done.2 = f32[80,4,256]{2,0,1:T(8,128)S(1)} async-done(((f32[80,4,256]{2,0,1:T(8,128)}), f32[80,4,256]{2,0,1:T(8,128)S(1)}, u32[]{:S(2)}, u32[]{:S(2)}) %all-to-all-start.2) | async-done | bytes 327712 | tf_op jit(solution)/shard_map/all_to_all | solution.py:163
  112.9 6.3 %scatter_custom_fusion = f32[80,2048]{0,1:T(8,128)S(1)} fusion(s32[1024]{0:T(1024)S(1)} %bitcast.147, f32[1024,80]{1,0:T(8,128)S(1)} %copy.109, f32[]{:T(128)} %constant.109.clone.1), kind=kCustom, calls=%fused_computation.92 | custom fusion | flops 81920 | bytes 655364 | tf_op jit(solution)/shard_map/scatter-add | solution.py:164
  (172 shorter events, 40.3 us)
Async XLA Ops:
  0.6 33.1 %copy-start = (f32[80,80]{1,0:T(8,128)S(1)}, f32[80,80]{1,0:T(8,128)}, u32[]{:S(2)}) copy-start(f32[80,80]{1,0:T(8,128)} %param.16) | copy-start | bytes 76804
  0.6 10.2 %copy-start.15 = (bf16[80,6,384]{2,0,1:T(8,128)(2,1)S(1)}, bf16[80,6,384]{2,0,1:T(8,128)(2,1)}, u32[]{:S(2)}) copy-start(bf16[80,6,384]{2,0,1:T(8,128)(2,1)} %param.11) | copy-start | bytes 1105924
  0.7 10.3 %copy-start.14 = (bf16[80,8,256]{2,1,0:T(8,128)(2,1)S(1)}, bf16[80,8,256]{2,1,0:T(8,128)(2,1)}, u32[]{:S(2)}) copy-start(bf16[80,8,256]{2,1,0:T(8,128)(2,1)} %param.10) | copy-start | bytes 983044
  3.5 14.6 %copy-start.20 = (s32[1,1,256,1]{2,3,1,0:T(1,128)S(1)}, s32[1,1,256,1]{2,3,1,0:T(1,128)}, u32[]{:S(2)}) copy-start(s32[1,1,256,1]{2,3,1,0:T(1,128)} %param.17) | copy-start | bytes 3076
  3.5 14.6 %copy-start.21 = (s32[1,1,256]{2,1,0:T(1,128)S(1)}, s32[1,1,256]{2,1,0:T(1,128)}, u32[]{:S(2)}) copy-start(s32[1,1,256]{2,1,0:T(1,128)} %param.18) | copy-start | bytes 3076
  3.5 28.7 %collective-permute-start = (bf16[80,640]{1,0:T(8,128)(2,1)}, bf16[80,640]{1,0:T(8,128)(2,1)}, u32[]{:S(2)}, u32[]{:S(2)}) collective-permute-start(bf16[80,640]{1,0:T(8,128)(2,1)} %pad_maximum_fusion), channel_id=1, source_target_pairs={{4,0},{8,4},{12,8},{5,1},{9,5},{13,9},{6,2},{10,6},{14,10},{7,3},{... | collective-permute-start | bytes 307208 | tf_op jit(solution)/shard_map/ppermute | solution.py:24
  5.6 27.4 %collective-permute-start.1 = (bf16[80,640]{1,0:T(8,128)(2,1)}, bf16[80,640]{1,0:T(8,128)(2,1)}, u32[]{:S(2)}, u32[]{:S(2)}) collective-permute-start(bf16[80,640]{1,0:T(8,128)(2,1)} %pad_maximum_fusion.1), channel_id=1, source_target_pairs={{0,4},{4,8},{8,12},{1,5},{5,9},{9,13},{2,6},{6,10},{10,14},{3,7},{... | collective-permute-start | bytes 307208 | tf_op jit(solution)/shard_map/ppermute | solution.py:23
  11.4 18.1 %collective-permute-start.3 = (bf16[80,14]{0,1:T(8,128)(2,1)S(1)}, bf16[80,14]{0,1:T(8,128)(2,1)S(1)}, u32[]{:S(2)}, u32[]{:S(2)}) collective-permute-start(bf16[80,14]{0,1:T(8,128)(2,1)S(1)} %pad_maximum_fusion.3), channel_id=1, source_target_pairs={{0,1},{1,2},{2,3},{4,5},{5,6},{6,7},{8,9},{9,10},{10,11},{12,13},{... | collective-permute-start | bytes 6728 | tf_op jit(solution)/shard_map/ppermute | solution.py:25
  16.1 13.4 %collective-permute-start.2 = (bf16[80,14]{0,1:T(8,128)(2,1)S(1)}, bf16[80,14]{0,1:T(8,128)(2,1)S(1)}, u32[]{:S(2)}, u32[]{:S(2)}) collective-permute-start(bf16[80,14]{0,1:T(8,128)(2,1)S(1)} %pad_maximum_fusion.2), channel_id=1, source_target_pairs={{1,0},{2,1},{3,2},{5,4},{6,5},{7,6},{9,8},{10,9},{11,10},{13,12},{... | collective-permute-start | bytes 6728 | tf_op jit(solution)/shard_map/ppermute | solution.py:26
  18.7 13.4 %all-to-all-start = ((s32[4,256,1]{1,2,0:T(1,128)}), s32[4,256,1]{1,2,0:T(1,128)S(1)}, u32[]{:S(2)}, u32[]{:S(2)}) async-start(s32[4,256,1]{1,2,0:T(1,128)} %compare_select_fusion.1), calls=%async_computation | async-start | bytes 8192 | tf_op jit(solution)/shard_map/all_to_all | solution.py:120
  40.7 14.1 %all-to-all-start.1 = ((f32[80,4,256]{2,0,1:T(8,128)}), f32[80,4,256]{2,0,1:T(8,128)S(1)}, u32[]{:S(2)}, u32[]{:S(2)}) async-start(f32[80,4,256]{2,0,1:T(8,128)} %broadcast_select_fusion.1), calls=%async_computation.1 | async-start | bytes 655360 | tf_op jit(solution)/shard_map/all_to_all | solution.py:121
  46.8 8.0 %copy-start.4 = (pred[256,2304]{1,0:T(32,128)(4,1)S(1)}, pred[256,2304]{1,0:T(32,128)(4,1)}, u32[]{:S(2)}) copy-start(pred[256,2304]{1,0:T(32,128)(4,1)} %fusion.6) | copy-start | bytes 1769476
  49.3 6.4 %copy-start.6 = (f32[80,2303]{1,0:T(8,128)S(1)}, f32[80,2303]{1,0:T(8,128)}, u32[]{:S(2)}) copy-start(f32[80,2303]{1,0:T(8,128)} %get-tuple-element.21) | copy-start | bytes 2210884
  49.3 6.4 %copy-start.18 = (f32[80]{0:T(128)S(1)}, f32[80]{0:T(128)}, u32[]{:S(2)}) copy-start(f32[80]{0:T(128)} %param.14) | copy-start | bytes 964
  49.3 6.4 %copy-start.19 = (f32[80]{0:T(128)S(1)}, f32[80]{0:T(128)}, u32[]{:S(2)}) copy-start(f32[80]{0:T(128)} %param.13) | copy-start | bytes 964
  59.7 13.8 %collective-permute-start.5 = (bf16[80,384]{1,0:T(8,128)(2,1)S(1)}, bf16[80,384]{1,0:T(8,128)(2,1)S(1)}, u32[]{:S(2)}, u32[]{:S(2)}) collective-permute-start(bf16[80,384]{1,0:T(8,128)(2,1)S(1)} %bitcast.142), channel_id=1, source_target_pairs={{0,4},{4,8},{8,12},{1,5},{5,9},{9,13},{2,6},{6,10},{10,14},{3,7},{... | collective-permute-start | bytes 184328 | tf_op jit(solution)/shard_map/ppermute | solution.py:23
  61.1 12.5 %collective-permute-start.4 = (bf16[80,384]{1,0:T(8,128)(2,1)S(1)}, bf16[80,384]{1,0:T(8,128)(2,1)S(1)}, u32[]{:S(2)}, u32[]{:S(2)}) collective-permute-start(bf16[80,384]{1,0:T(8,128)(2,1)S(1)} %bitcast.144), channel_id=1, source_target_pairs={{4,0},{8,4},{12,8},{5,1},{9,5},{13,9},{6,2},{10,6},{14,10},{7,3},{... | collective-permute-start | bytes 184328 | tf_op jit(solution)/shard_map/ppermute | solution.py:24
  62.5 8.7 %collective-permute-start.7 = (bf16[80,6]{0,1:T(8,128)(2,1)S(1)}, bf16[80,6]{0,1:T(8,128)(2,1)S(1)}, u32[]{:S(2)}, u32[]{:S(2)}) collective-permute-start(bf16[80,6]{0,1:T(8,128)(2,1)S(1)} %bitcast.154), channel_id=1, source_target_pairs={{0,1},{1,2},{2,3},{4,5},{5,6},{6,7},{8,9},{9,10},{10,11},{12,13},{... | collective-permute-start | bytes 2888 | tf_op jit(solution)/shard_map/ppermute | solution.py:25
  68.2 4.9 %collective-permute-start.6 = (bf16[80,6]{0,1:T(8,128)(2,1)S(1)}, bf16[80,6]{0,1:T(8,128)(2,1)S(1)}, u32[]{:S(2)}, u32[]{:S(2)}) collective-permute-start(bf16[80,6]{0,1:T(8,128)(2,1)S(1)} %bitcast.156), channel_id=1, source_target_pairs={{1,0},{2,1},{3,2},{5,4},{6,5},{7,6},{9,8},{10,9},{11,10},{13,12},{... | collective-permute-start | bytes 2888 | tf_op jit(solution)/shard_map/ppermute | solution.py:26
  77.0 16.3 %collective-permute-start.9 = (bf16[80,384]{1,0:T(8,128)(2,1)S(1)}, bf16[80,384]{1,0:T(8,128)(2,1)}, u32[]{:S(2)}, u32[]{:S(2)}) collective-permute-start(bf16[80,384]{1,0:T(8,128)(2,1)S(1)} %bitcast.143), channel_id=1, source_target_pairs={{0,4},{4,8},{8,12},{1,5},{5,9},{9,13},{2,6},{6,10},{10,14},{3,7},{... | collective-permute-start | bytes 184328 | tf_op jit(solution)/shard_map/ppermute | solution.py:23
  82.5 11.7 %collective-permute-start.8 = (bf16[80,384]{1,0:T(8,128)(2,1)}, bf16[80,384]{1,0:T(8,128)(2,1)}, u32[]{:S(2)}, u32[]{:S(2)}) collective-permute-start(bf16[80,384]{1,0:T(8,128)(2,1)} %bitcast.105), channel_id=1, source_target_pairs={{4,0},{8,4},{12,8},{5,1},{9,5},{13,9},{6,2},{10,6},{14,10},{7,3},{... | collective-permute-start | bytes 184328 | tf_op jit(solution)/shard_map/ppermute | solution.py:24
  84.2 6.8 %collective-permute-start.11 = (bf16[80,6]{0,1:T(8,128)(2,1)S(1)}, bf16[80,6]{0,1:T(8,128)(2,1)S(1)}, u32[]{:S(2)}, u32[]{:S(2)}) collective-permute-start(bf16[80,6]{0,1:T(8,128)(2,1)S(1)} %bitcast.155), channel_id=1, source_target_pairs={{0,1},{1,2},{2,3},{4,5},{5,6},{6,7},{8,9},{9,10},{10,11},{12,13},{... | collective-permute-start | bytes 2888 | tf_op jit(solution)/shard_map/ppermute | solution.py:25
  87.9 4.9 %collective-permute-start.10 = (bf16[80,6]{0,1:T(8,128)(2,1)S(1)}, bf16[80,6]{0,1:T(8,128)(2,1)S(1)}, u32[]{:S(2)}, u32[]{:S(2)}) collective-permute-start(bf16[80,6]{0,1:T(8,128)(2,1)S(1)} %bitcast.157), channel_id=1, source_target_pairs={{1,0},{2,1},{3,2},{5,4},{6,5},{7,6},{9,8},{10,9},{11,10},{13,12},{... | collective-permute-start | bytes 2888 | tf_op jit(solution)/shard_map/ppermute | solution.py:26
  98.5 14.2 %all-to-all-start.2 = ((f32[80,4,256]{2,0,1:T(8,128)}), f32[80,4,256]{2,0,1:T(8,128)S(1)}, u32[]{:S(2)}, u32[]{:S(2)}) async-start(f32[80,4,256]{2,0,1:T(8,128)} %broadcast_select_fusion), calls=%async_computation.2 | async-start | bytes 655360 | tf_op jit(solution)/shard_map/all_to_all | solution.py:163
  (15 other events, 24.0 us)
where the time goes:
time: 122 us; the launch traced here: 121 us
  starting transfers between devices  46.3 us (38%)
  local copies, waits for them, and re-layouts  30.1 us (25%)
  other arithmetic  18.7 us (15%)
  waiting for transfers between devices  13.9 us (11%)
  matrix products  10.8 us (9%)
  between operations  1.45 us (1%)
    ppermute x3, starting transfers between devices, exchange(): left = lax.ppermute(last_cols, Y_AXES, fwd_y)  12.1 us
    ppermute x3, starting transfers between devices, exchange(): above = lax.ppermute(last_rows, 'gx', fwd_x)  11.5 us
    unnamed x68, local copies, waits for them, and re-layouts  10.8 us
    all_to_all x1, waiting for transfers between devices, body(): lax.all_to_all(outgoing, 'gx', split_axis=1, concat_axis=1, tiled=True)  8.71 us
    dot_general x4, matrix products, mix_levels(): jnp.dot(matrix, flat, precision=HI, preferred_element_type=jnp.float32)  8.71 us
    convert_element_type x12, other arithmetic, flat_stencil(): above, below, left, right = (h.astype(flat.dtype) for h in halo)  6.43 us
    scatter-add x1, other arithmetic, body(): summed = jnp.zeros_like(flat_parent).at[:, served_ids].add(incoming)  6.28 us
    ppermute x3, starting transfers between devices, exchange(): right = lax.ppermute(first_cols, Y_AXES, bwd_y)  5.74 us
  transfers between devices with their start and end apart: 15, of which 4 were waited for; matrix products, arithmetic and copies ran while one was open for 23% of the time, Pallas kernels for 0%

commit v1 on v0

--- a/solution.py
+++ b/solution.py
@@ -5,6 +5,18 @@
 
 Y_AXES = ("gy", "gz")
 HI = lax.Precision.HIGHEST
+
+
+def in_blocks(value, dim, size):
+    shape = value.shape
+    parts = value.reshape(*shape[:dim], size, shape[dim] // size, *shape[dim + 1 :])
+    return jnp.moveaxis(parts, dim, 0)
+
+
+def joined_along(blocks, dim):
+    blocks = jnp.moveaxis(blocks, 0, dim)
+    dims = blocks.shape
+    return blocks.reshape(*dims[:dim], dims[dim] * dims[dim + 1], *dims[dim + 2 :])
 
 
 def shift_pairs(count):
@@ -118,9 +130,17 @@
         places = owners * slots + order_in
         wanted = jnp.zeros((tiles_x * slots,), jnp.int32).at[places].set(cells)
     served_ids = lax.all_to_all(wanted, "gx", split_axis=0, concat_axis=0, tiled=True)
-    answers = lax.all_to_all(
-        jnp.take(flat_parent, served_ids, axis=1), "gx", split_axis=1, concat_axis=1, tiled=True
-    )
+    shard = jnp.take(flat_parent, served_ids, axis=1)
+    devices, index = (lax.axis_size("gx"), lax.axis_index("gx"))
+    blocks_2 = in_blocks(shard, 1, devices)
+    outs = [blocks_2[index]]
+    for hop in range(1, devices):
+        sent = blocks_2[(index + hop) % devices]
+        outs.append(
+            lax.ppermute(sent, "gx", [(i_2, (i_2 + hop) % devices) for i_2 in range(devices)])
+        )
+    blocks_2 = jnp.stack(outs)[(index - jnp.arange(devices)) % devices]
+    answers = joined_along(blocks_2, 1)
     if slots >= requests:
         answers = answers.reshape(levels, tiles_x, slots)[:, :, :requests]
         forcing_flat = answers[:, 0, :]

time: 122 us -> 118 us (0.967)
  other arithmetic: 18.7 us -> 11.9 us
  local copies, waits for them, and re-layouts: 30.1 us -> 32.6 us
    convert_element_type x12, other arithmetic: 6.43 us -> 1.39 us  [flat_stencil(): above, below, left, right = (h.astype(flat.dtype) for h in halo)]
    ppermute x0 -> x3, starting transfers between devices: none -> 4.9 us  [body(): lax.ppermute(sent, 'gx', [(i_2, (i_2 + hop) % devices) for i_2 in range(d...]
    all_to_all x1 -> x0, starting transfers between devices: 4.54 us -> none  [body(): lax.all_to_all(jnp.take(flat_parent, served_ids, axis=1), 'gx', split_axi...]
    all_to_all x1 -> x0, waiting for transfers between devices: 3.94 us -> none  [body(): lax.all_to_all(jnp.take(flat_parent, served_ids, axis=1), 'gx', split_axi...]
    ppermute x0 -> x3, waiting for transfers between devices: none -> 3.24 us  [body(): lax.ppermute(sent, 'gx', [(i_2, (i_2 + hop) % devices) for i_2 in range(d...]
    slice x6, local copies, waits for them, and re-layouts: 0.79 us -> 2.83 us  [exchange(): first_cols = jnp.concatenate([b[:, :, 0] for b in blocks], axis=1)]
    all_to_all x1, starting transfers between devices: 3.58 us -> 5.38 us  [body(): lax.all_to_all(wanted, 'gx', split_axis=0, concat_axis=0, tiled=True)]
    unnamed x68 -> x80, local copies, waits for them, and re-layouts: 10.8 us -> 12.5 us
  transfers between devices with their start and end apart: 15 -> 17, of which waited for: 4 -> 2; matrix products, arithmetic and copies ran while one was open for 23% -> 20% of each run, Pallas kernels for 0% -> 0%
where the time goes in v1:
time: 118 us; the launch traced here: 116 us
  starting transfers between devices  47.1 us (40%)
  local copies, waits for them, and re-layouts  32.6 us (28%)
  waiting for transfers between devices  12.9 us (11%)
  other arithmetic  11.9 us (10%)
  matrix products  10.3 us (9%)
  between operations  1.65 us (1%)
    unnamed x80, local copies, waits for them, and re-layouts  12.5 us
    ppermute x3, starting transfers between devices, exchange(): above = lax.ppermute(last_rows, 'gx', fwd_x)  11.9 us
    ppermute x3, starting transfers between devices, exchange(): left = lax.ppermute(last_cols, Y_AXES, fwd_y)  10.9 us
    all_to_all x1, waiting for transfers between devices, body(): lax.all_to_all(outgoing, 'gx', split_axis=1, concat_axis=1, tiled=True)  9.61 us
    dot_general x4, matrix products, mix_levels(): jnp.dot(matrix, flat, precision=HI, preferred_element_type=jnp.float32)  8.25 us
    ppermute x3, starting transfers between devices, exchange(): right = lax.ppermute(first_cols, Y_AXES, bwd_y)  6.58 us
    scatter-add x1, other arithmetic, body(): summed = jnp.zeros_like(flat_parent).at[:, served_ids].add(incoming)  6.28 us
    all_to_all x1, starting transfers between devices, body(): lax.all_to_all(wanted, 'gx', split_axis=0, concat_axis=0, tiled=True)  5.38 us
  transfers between devices with their start and end apart: 17, of which 2 were waited for; matrix products, arithmetic and copies ran while one was open for 20% of the time, Pallas kernels for 0%

profile of v1, /device:TPU:1, one launch (start us, length us, event | category | flops | bytes accessed | tf_op | source)
XLA Modules:
  0.0 116.4 jit_solution(6867547979093723645)
XLA Ops:
  3.3 1.9 %collective-permute-start.2 = (bf16[80,14]{0,1:T(8,128)(2,1)S(1)}, bf16[80,14]{0,1:T(8,128)(2,1)S(1)}, u32[]{:S(2)}, u32[]{:S(2)}) collective-permute-start(bf16[80,14]{0,1:T(8,128)(2,1)S(1)} %pad_maximum_fusion.3), channel_id=1, source_target_pairs={{1,0},{2,1},{3,2},{5,4},{6,5},{7,6},{9,8},{10,9},{11,10},{13,12},{... | collective-permute-start | bytes 6728 | tf_op jit(solution)/shard_map/ppermute | solution.py:38
  5.5 4.5 %collective-permute-start.3 = (bf16[80,14]{0,1:T(8,128)(2,1)S(1)}, bf16[80,14]{0,1:T(8,128)(2,1)S(1)}, u32[]{:S(2)}, u32[]{:S(2)}) collective-permute-start(bf16[80,14]{0,1:T(8,128)(2,1)S(1)} %pad_maximum_fusion.4), channel_id=1, source_target_pairs={{0,1},{1,2},{2,3},{4,5},{5,6},{6,7},{8,9},{9,10},{10,11},{12,13},{... | collective-permute-start | bytes 6728 | tf_op jit(solution)/shard_map/ppermute | solution.py:37
  10.2 3.2 %collective-permute-start.1 = (bf16[80,640]{1,0:T(8,128)(2,1)S(1)}, bf16[80,640]{1,0:T(8,128)(2,1)S(1)}, u32[]{:S(2)}, u32[]{:S(2)}) collective-permute-start(bf16[80,640]{1,0:T(8,128)(2,1)S(1)} %pad_maximum_fusion.2), channel_id=1, source_target_pairs={{0,4},{4,8},{8,12},{1,5},{5,9},{9,13},{2,6},{6,10},{10,14},{3,7},{... | collective-permute-start | bytes 307208 | tf_op jit(solution)/shard_map/ppermute | solution.py:35
  13.5 1.3 %collective-permute-start = (bf16[80,640]{1,0:T(8,128)(2,1)S(1)}, bf16[80,640]{1,0:T(8,128)(2,1)S(1)}, u32[]{:S(2)}, u32[]{:S(2)}) collective-permute-start(bf16[80,640]{1,0:T(8,128)(2,1)S(1)} %pad_maximum_fusion.1), channel_id=1, source_target_pairs={{4,0},{8,4},{12,8},{5,1},{9,5},{13,9},{6,2},{10,6},{14,10},{7,3},{... | collective-permute-start | bytes 307208 | tf_op jit(solution)/shard_map/ppermute | solution.py:36
  15.4 5.4 %all-to-all-start = ((s32[4,256,1]{1,2,0:T(1,128)}), s32[4,256,1]{1,2,0:T(1,128)S(1)}, u32[]{:S(2)}, u32[]{:S(2)}) async-start(s32[4,256,1]{1,2,0:T(1,128)} %compare_select_fusion.1), calls=%async_computation | async-start | bytes 8192 | tf_op jit(solution)/shard_map/all_to_all | solution.py:132
  22.4 1.4 %fusion.136 = (f32[80,2303]{1,0:T(8,128)}, f32[80,2303]{1,0:T(8,128)}) fusion(f32[80,2304]{1,0:T(8,128)S(1)} %bitcast.120), kind=kLoop, calls=%fused_computation.223 | loop fusion | bytes 2947840 | tf_op jit(solution)/shard_map/slice | solution.py:76
  25.8 2.2 %fusion.6 = pred[256,2304]{1,0:T(32,128)(4,1)} fusion(s32[256]{0:T(256)S(1)} %get-tuple-element.62, s32[256]{0:T(256)S(1)} %get-tuple-element.63, s32[2304]{0:T(1024)S(1)} %get-tuple-element.66, s32[2304]{0:T(1024)S(1)} %get-tuple-element.67, s32[256]{0:T(256)S(1)} %get-tuple-element.61, s32[256]{0:T(256)S(1)} %get-tuple-element.64, ...), kind=kLoop, calls=%fused_computation.21 | loop fusion | flops 13565952 | bytes 635904 | tf_op jit(solution)/shard_map/and | solution.py:103
  34.0 2.8 %convolution_bitcast_fusion.2 = f32[80,2048]{1,0:T(8,128)S(1)} fusion(f32[80,80]{1,0:T(8,128)S(1)} %copy-done, f32[80,2048]{1,0:T(8,128)S(1)} %bitcast.125, f32[80,256]{1,0:T(8,128)S(1)} %slice_convert_fusion.3, f32[80,1792]{1,0:T(8,128)} %get-tuple-element.28, f32[80,1792]{1,0:T(8,128)} %get-tuple-element.27, f32[80,256]{1,0:T(8,128)S(1)} %slice_convert_fusion.2, ...), kind=kOutput, calls=%fused_computation.14 | convolution fusion | flops 159088640 | bytes 5272256 | tf_op jit(solution)/shard_map/dot_general | solution.py:85
  37.1 2.8 %gather_fusion.1 = f32[1024,80]{1,0:T(8,128)S(1)} fusion(f32[80,2048]{0,1:T(8,128)S(1)} %copy.97, s32[1024]{0:T(1024)S(1)} %broadcast_clamp_fusion), kind=kCustom, calls=%fused_computation.1 | custom fusion | bytes 659456 | tf_op jit(solution)/shard_map/jit(_take)/gather | solution.py:133
  40.3 1.5 %collective-permute-start.4 = (f32[80,256]{1,0:T(8,128)S(1)}, f32[80,256]{1,0:T(8,128)S(1)}, u32[]{:S(2)}, u32[]{:S(2)}) collective-permute-start(f32[80,256]{1,0:T(8,128)S(1)} %bitcast.157), channel_id=1, source_target_pairs={{0,4},{4,8},{8,12},{12,0},{1,5},{5,9},{9,13},{13,1},{2,6},{6,10},{... | collective-permute-start | bytes 245768 | tf_op jit(solution)/shard_map/ppermute | solution.py:140
  41.9 2.1 %collective-permute-start.5 = (f32[80,256]{1,0:T(8,128)S(1)}, f32[80,256]{1,0:T(8,128)S(1)}, u32[]{:S(2)}, u32[]{:S(2)}) collective-permute-start(f32[80,256]{1,0:T(8,128)S(1)} %bitcast.158), channel_id=1, source_target_pairs={{0,8},{4,12},{8,0},{12,4},{1,9},{5,13},{9,1},{13,5},{2,10},{6,14},... | collective-permute-start | bytes 245768 | tf_op jit(solution)/shard_map/ppermute | solution.py:140
  46.8 3.2 %collective-permute-done.5 = f32[80,256]{1,0:T(8,128)S(1)} collective-permute-done((f32[80,256]{1,0:T(8,128)S(1)}, f32[80,256]{1,0:T(8,128)S(1)}, u32[]{:S(2)}, u32[]{:S(2)}) %collective-permute-start.5) | collective-permute-done | bytes 81952 | tf_op jit(solution)/shard_map/ppermute | solution.py:140
  52.1 2.8 %fusion.147 = (bf16[80,2304]{1,0:T(8,128)(2,1)S(1)}, f32[80,2304]{1,0:T(8,128)S(1)}) fusion(f32[80,80]{1,0:T(8,128)S(1)} %copy-done, f32[80,2304]{1,0:T(8,128)S(1)} %fusion.150, f32[80,2304]{1,0:T(8,128)S(1)} %bitcast.122, f32[80,1920]{1,0:T(8,128)} %get-tuple-element.23, f32[80,384]{1,0:T(8,128)S(1)} %copy-done.18, f32[80,384]{1,0:T(8,128)S(1)} %copy-done.19, ...), kind=kOutput, calls=%fused_computation.234 | convolution fusion | flops 180080640 | bytes 7052800 | tf_op jit(solution)/shard_map/dot_general | solution.py:85
  55.8 2.7 %collective-permute-start.9 = (bf16[80,6]{0,1:T(8,128)(2,1)S(1)}, bf16[80,6]{0,1:T(8,128)(2,1)S(1)}, u32[]{:S(2)}, u32[]{:S(2)}) collective-permute-start(bf16[80,6]{0,1:T(8,128)(2,1)S(1)} %bitcast.175), channel_id=1, source_target_pairs={{1,0},{2,1},{3,2},{5,4},{6,5},{7,6},{9,8},{10,9},{11,10},{13,12},{... | collective-permute-start | bytes 2888 | tf_op jit(solution)/shard_map/ppermute | solution.py:38
  58.7 2.8 %collective-permute-start.10 = (bf16[80,6]{0,1:T(8,128)(2,1)S(1)}, bf16[80,6]{0,1:T(8,128)(2,1)S(1)}, u32[]{:S(2)}, u32[]{:S(2)}) collective-permute-start(bf16[80,6]{0,1:T(8,128)(2,1)S(1)} %bitcast.173), channel_id=1, source_target_pairs={{0,1},{1,2},{2,3},{4,5},{5,6},{6,7},{8,9},{9,10},{10,11},{12,13},{... | collective-permute-start | bytes 2888 | tf_op jit(solution)/shard_map/ppermute | solution.py:37
  64.0 4.8 %collective-permute-start.8 = (bf16[80,384]{1,0:T(8,128)(2,1)S(1)}, bf16[80,384]{1,0:T(8,128)(2,1)S(1)}, u32[]{:S(2)}, u32[]{:S(2)}) collective-permute-start(bf16[80,384]{1,0:T(8,128)(2,1)S(1)} %bitcast.162), channel_id=1, source_target_pairs={{0,4},{4,8},{8,12},{1,5},{5,9},{9,13},{2,6},{6,10},{10,14},{3,7},{... | collective-permute-start | bytes 184328 | tf_op jit(solution)/shard_map/ppermute | solution.py:35
  73.0 1.3 %fusion.148 = (bf16[80,2304]{1,0:T(8,128)(2,1)S(1)}, f32[80,2304]{1,0:T(8,128)S(1)}) fusion(f32[80,80]{1,0:T(8,128)S(1)} %copy-done, f32[80,2304]{1,0:T(8,128)S(1)} %fusion.150, f32[80,2304]{1,0:T(8,128)S(1)} %get-tuple-element.52, f32[80,1920]{1,0:T(8,128)S(1)} %copy-done.14, f32[80,384]{1,0:T(8,128)S(1)} %convert_element_type.84, ...), kind=kOutput, calls=%fused_computation.235 | convolution fusion | flops 180080640 | bytes 7052800 | tf_op jit(solution)/shard_map/dot_general | solution.py:85
  75.2 1.9 %collective-permute-start.13 = (bf16[80,6]{0,1:T(8,128)(2,1)S(1)}, bf16[80,6]{0,1:T(8,128)(2,1)S(1)}, u32[]{:S(2)}, u32[]{:S(2)}) collective-permute-start(bf16[80,6]{0,1:T(8,128)(2,1)S(1)} %bitcast.176), channel_id=1, source_target_pairs={{1,0},{2,1},{3,2},{5,4},{6,5},{7,6},{9,8},{10,9},{11,10},{13,12},{... | collective-permute-start | bytes 2888 | tf_op jit(solution)/shard_map/ppermute | solution.py:38
  77.3 3.6 %collective-permute-start.14 = (bf16[80,6]{0,1:T(8,128)(2,1)S(1)}, bf16[80,6]{0,1:T(8,128)(2,1)S(1)}, u32[]{:S(2)}, u32[]{:S(2)}) collective-permute-start(bf16[80,6]{0,1:T(8,128)(2,1)S(1)} %bitcast.174), channel_id=1, source_target_pairs={{0,1},{1,2},{2,3},{4,5},{5,6},{6,7},{8,9},{9,10},{10,11},{12,13},{... | collective-permute-start | bytes 2888 | tf_op jit(solution)/shard_map/ppermute | solution.py:37
  82.5 4.0 %collective-permute-start.12 = (bf16[80,384]{1,0:T(8,128)(2,1)S(1)}, bf16[80,384]{1,0:T(8,128)(2,1)S(1)}, u32[]{:S(2)}, u32[]{:S(2)}) collective-permute-start(bf16[80,384]{1,0:T(8,128)(2,1)S(1)} %bitcast.163), channel_id=1, source_target_pairs={{0,4},{4,8},{8,12},{1,5},{5,9},{9,13},{2,6},{6,10},{10,14},{3,7},{... | collective-permute-start | bytes 184328 | tf_op jit(solution)/shard_map/ppermute | solution.py:35
  90.7 1.3 %fusion.149 = (bf16[2304,80]{0,1:T(8,128)(2,1)S(1)}, f32[2304,80]{0,1:T(8,128)S(1)}) fusion(f32[80,80]{1,0:T(8,128)S(1)} %copy-done, f32[80,2304]{1,0:T(8,128)S(1)} %fusion.150, f32[80,2304]{1,0:T(8,128)S(1)} %get-tuple-element.54, f32[80,1920]{1,0:T(8,128)S(1)} %copy-done.12, f32[80,384]{1,0:T(8,128)S(1)} %convert_element_type.89, ...), kind=kOutput, calls=%fused_computation.236 | convolution fusion | flops 180080640 | bytes 7052800 | tf_op jit(solution)/shard_map/dot_general | solution.py:85
  94.0 3.5 %all-to-all-start.1 = ((f32[80,4,256]{2,0,1:T(8,128)}), f32[80,4,256]{2,0,1:T(8,128)S(1)}, u32[]{:S(2)}, u32[]{:S(2)}) async-start(f32[80,4,256]{2,0,1:T(8,128)} %broadcast_select_fusion.1), calls=%async_computation.1 | async-start | bytes 655360 | tf_op jit(solution)/shard_map/all_to_all | solution.py:183
  98.3 9.6 %all-to-all-done.1 = f32[80,4,256]{2,0,1:T(8,128)S(1)} async-done(((f32[80,4,256]{2,0,1:T(8,128)}), f32[80,4,256]{2,0,1:T(8,128)S(1)}, u32[]{:S(2)}, u32[]{:S(2)}) %all-to-all-start.1) | async-done | bytes 327712 | tf_op jit(solution)/shard_map/all_to_all | solution.py:183
  108.1 6.3 %scatter_custom_fusion = f32[80,2048]{0,1:T(8,128)S(1)} fusion(s32[1024]{0:T(1024)S(1)} %bitcast.166, f32[1024,80]{1,0:T(8,128)S(1)} %copy.115, f32[]{:T(128)} %constant.138.clone.1), kind=kCustom, calls=%fused_computation.93 | custom fusion | flops 81920 | bytes 655364 | tf_op jit(solution)/shard_map/scatter-add | solution.py:184
  (196 shorter events, 37.8 us)
Async XLA Ops:
  0.6 33.3 %copy-start = (f32[80,80]{1,0:T(8,128)S(1)}, f32[80,80]{1,0:T(8,128)}, u32[]{:S(2)}) copy-start(f32[80,80]{1,0:T(8,128)} %param.16) | copy-start | bytes 76804
  0.6 9.4 %copy-start.16 = (bf16[80,8,256]{2,1,0:T(8,128)(2,1)S(1)}, bf16[80,8,256]{2,1,0:T(8,128)(2,1)}, u32[]{:S(2)}) copy-start(bf16[80,8,256]{2,1,0:T(8,128)(2,1)} %param.10) | copy-start | bytes 983044
  0.7 9.5 %copy-start.17 = (bf16[80,6,384]{2,0,1:T(8,128)(2,1)S(1)}, bf16[80,6,384]{2,0,1:T(8,128)(2,1)}, u32[]{:S(2)}) copy-start(bf16[80,6,384]{2,0,1:T(8,128)(2,1)} %param.11) | copy-start | bytes 1105924
  2.0 12.7 %copy-start.26 = (s32[1,1,256,1]{2,3,1,0:T(1,128)S(1)}, s32[1,1,256,1]{2,3,1,0:T(1,128)}, u32[]{:S(2)}) copy-start(s32[1,1,256,1]{2,3,1,0:T(1,128)} %param.17) | copy-start | bytes 3076
  2.0 12.8 %copy-start.27 = (s32[1,1,256]{2,1,0:T(1,128)S(1)}, s32[1,1,256]{2,1,0:T(1,128)}, u32[]{:S(2)}) copy-start(s32[1,1,256]{2,1,0:T(1,128)} %param.18) | copy-start | bytes 3076
  3.3 24.8 %collective-permute-start.2 = (bf16[80,14]{0,1:T(8,128)(2,1)S(1)}, bf16[80,14]{0,1:T(8,128)(2,1)S(1)}, u32[]{:S(2)}, u32[]{:S(2)}) collective-permute-start(bf16[80,14]{0,1:T(8,128)(2,1)S(1)} %pad_maximum_fusion.3), channel_id=1, source_target_pairs={{1,0},{2,1},{3,2},{5,4},{6,5},{7,6},{9,8},{10,9},{11,10},{13,12},{... | collective-permute-start | bytes 6728 | tf_op jit(solution)/shard_map/ppermute | solution.py:38
  5.5 22.6 %collective-permute-start.3 = (bf16[80,14]{0,1:T(8,128)(2,1)S(1)}, bf16[80,14]{0,1:T(8,128)(2,1)S(1)}, u32[]{:S(2)}, u32[]{:S(2)}) collective-permute-start(bf16[80,14]{0,1:T(8,128)(2,1)S(1)} %pad_maximum_fusion.4), channel_id=1, source_target_pairs={{0,1},{1,2},{2,3},{4,5},{5,6},{6,7},{8,9},{9,10},{10,11},{12,13},{... | collective-permute-start | bytes 6728 | tf_op jit(solution)/shard_map/ppermute | solution.py:37
  10.2 23.1 %collective-permute-start.1 = (bf16[80,640]{1,0:T(8,128)(2,1)S(1)}, bf16[80,640]{1,0:T(8,128)(2,1)S(1)}, u32[]{:S(2)}, u32[]{:S(2)}) collective-permute-start(bf16[80,640]{1,0:T(8,128)(2,1)S(1)} %pad_maximum_fusion.2), channel_id=1, source_target_pairs={{0,4},{4,8},{8,12},{1,5},{5,9},{9,13},{2,6},{6,10},{10,14},{3,7},{... | collective-permute-start | bytes 307208 | tf_op jit(solution)/shard_map/ppermute | solution.py:35
  13.5 19.8 %collective-permute-start = (bf16[80,640]{1,0:T(8,128)(2,1)S(1)}, bf16[80,640]{1,0:T(8,128)(2,1)S(1)}, u32[]{:S(2)}, u32[]{:S(2)}) collective-permute-start(bf16[80,640]{1,0:T(8,128)(2,1)S(1)} %pad_maximum_fusion.1), channel_id=1, source_target_pairs={{4,0},{8,4},{12,8},{5,1},{9,5},{13,9},{6,2},{10,6},{14,10},{7,3},{... | collective-permute-start | bytes 307208 | tf_op jit(solution)/shard_map/ppermute | solution.py:36
  15.4 17.8 %all-to-all-start = ((s32[4,256,1]{1,2,0:T(1,128)}), s32[4,256,1]{1,2,0:T(1,128)S(1)}, u32[]{:S(2)}, u32[]{:S(2)}) async-start(s32[4,256,1]{1,2,0:T(1,128)} %compare_select_fusion.1), calls=%async_computation | async-start | bytes 8192 | tf_op jit(solution)/shard_map/all_to_all | solution.py:132
  40.1 5.2 %copy-start.21 = (bf16[80,640]{1,0:T(8,128)(2,1)S(1)}, bf16[80,640]{1,0:T(8,128)(2,1)}, u32[]{:S(2)}) copy-start(bf16[80,640]{1,0:T(8,128)(2,1)} %copy-done.20) | copy-start | bytes 307204
  40.1 5.9 %copy-start.23 = (bf16[80,640]{1,0:T(8,128)(2,1)S(1)}, bf16[80,640]{1,0:T(8,128)(2,1)}, u32[]{:S(2)}) copy-start(bf16[80,640]{1,0:T(8,128)(2,1)} %copy-done.22) | copy-start | bytes 307204
  40.3 6.5 %collective-permute-start.4 = (f32[80,256]{1,0:T(8,128)S(1)}, f32[80,256]{1,0:T(8,128)S(1)}, u32[]{:S(2)}, u32[]{:S(2)}) collective-permute-start(f32[80,256]{1,0:T(8,128)S(1)} %bitcast.157), channel_id=1, source_target_pairs={{0,4},{4,8},{8,12},{12,0},{1,5},{5,9},{9,13},{13,1},{2,6},{6,10},{... | collective-permute-start | bytes 245768 | tf_op jit(solution)/shard_map/ppermute | solution.py:140
  41.9 8.1 %collective-permute-start.5 = (f32[80,256]{1,0:T(8,128)S(1)}, f32[80,256]{1,0:T(8,128)S(1)}, u32[]{:S(2)}, u32[]{:S(2)}) collective-permute-start(f32[80,256]{1,0:T(8,128)S(1)} %bitcast.158), channel_id=1, source_target_pairs={{0,8},{4,12},{8,0},{12,4},{1,9},{5,13},{9,1},{13,5},{2,10},{6,14},... | collective-permute-start | bytes 245768 | tf_op jit(solution)/shard_map/ppermute | solution.py:140
  44.1 5.9 %collective-permute-start.6 = (f32[80,256]{1,0:T(8,128)S(1)}, f32[80,256]{1,0:T(8,128)S(1)}, u32[]{:S(2)}, u32[]{:S(2)}) collective-permute-start(f32[80,256]{1,0:T(8,128)S(1)} %bitcast.159), channel_id=1, source_target_pairs={{0,12},{4,0},{8,4},{12,8},{1,13},{5,1},{9,5},{13,9},{2,14},{6,2},{... | collective-permute-start | bytes 245768 | tf_op jit(solution)/shard_map/ppermute | solution.py:140
  55.8 14.1 %collective-permute-start.9 = (bf16[80,6]{0,1:T(8,128)(2,1)S(1)}, bf16[80,6]{0,1:T(8,128)(2,1)S(1)}, u32[]{:S(2)}, u32[]{:S(2)}) collective-permute-start(bf16[80,6]{0,1:T(8,128)(2,1)S(1)} %bitcast.175), channel_id=1, source_target_pairs={{1,0},{2,1},{3,2},{5,4},{6,5},{7,6},{9,8},{10,9},{11,10},{13,12},{... | collective-permute-start | bytes 2888 | tf_op jit(solution)/shard_map/ppermute | solution.py:38
  58.7 12.4 %collective-permute-start.10 = (bf16[80,6]{0,1:T(8,128)(2,1)S(1)}, bf16[80,6]{0,1:T(8,128)(2,1)S(1)}, u32[]{:S(2)}, u32[]{:S(2)}) collective-permute-start(bf16[80,6]{0,1:T(8,128)(2,1)S(1)} %bitcast.173), channel_id=1, source_target_pairs={{0,1},{1,2},{2,3},{4,5},{5,6},{6,7},{8,9},{9,10},{10,11},{12,13},{... | collective-permute-start | bytes 2888 | tf_op jit(solution)/shard_map/ppermute | solution.py:37
  62.7 8.9 %collective-permute-start.7 = (bf16[80,384]{1,0:T(8,128)(2,1)S(1)}, bf16[80,384]{1,0:T(8,128)(2,1)S(1)}, u32[]{:S(2)}, u32[]{:S(2)}) collective-permute-start(bf16[80,384]{1,0:T(8,128)(2,1)S(1)} %bitcast.160), channel_id=1, source_target_pairs={{4,0},{8,4},{12,8},{5,1},{9,5},{13,9},{6,2},{10,6},{14,10},{7,3},{... | collective-permute-start | bytes 184328 | tf_op jit(solution)/shard_map/ppermute | solution.py:36
  64.0 7.6 %collective-permute-start.8 = (bf16[80,384]{1,0:T(8,128)(2,1)S(1)}, bf16[80,384]{1,0:T(8,128)(2,1)S(1)}, u32[]{:S(2)}, u32[]{:S(2)}) collective-permute-start(bf16[80,384]{1,0:T(8,128)(2,1)S(1)} %bitcast.162), channel_id=1, source_target_pairs={{0,4},{4,8},{8,12},{1,5},{5,9},{9,13},{2,6},{6,10},{10,14},{3,7},{... | collective-permute-start | bytes 184328 | tf_op jit(solution)/shard_map/ppermute | solution.py:35
  75.2 12.4 %collective-permute-start.13 = (bf16[80,6]{0,1:T(8,128)(2,1)S(1)}, bf16[80,6]{0,1:T(8,128)(2,1)S(1)}, u32[]{:S(2)}, u32[]{:S(2)}) collective-permute-start(bf16[80,6]{0,1:T(8,128)(2,1)S(1)} %bitcast.176), channel_id=1, source_target_pairs={{1,0},{2,1},{3,2},{5,4},{6,5},{7,6},{9,8},{10,9},{11,10},{13,12},{... | collective-permute-start | bytes 2888 | tf_op jit(solution)/shard_map/ppermute | solution.py:38
  77.3 11.7 %collective-permute-start.14 = (bf16[80,6]{0,1:T(8,128)(2,1)S(1)}, bf16[80,6]{0,1:T(8,128)(2,1)S(1)}, u32[]{:S(2)}, u32[]{:S(2)}) collective-permute-start(bf16[80,6]{0,1:T(8,128)(2,1)S(1)} %bitcast.174), channel_id=1, source_target_pairs={{0,1},{1,2},{2,3},{4,5},{5,6},{6,7},{8,9},{9,10},{10,11},{12,13},{... | collective-permute-start | bytes 2888 | tf_op jit(solution)/shard_map/ppermute | solution.py:37
  81.2 8.2 %collective-permute-start.11 = (bf16[80,384]{1,0:T(8,128)(2,1)S(1)}, bf16[80,384]{1,0:T(8,128)(2,1)S(1)}, u32[]{:S(2)}, u32[]{:S(2)}) collective-permute-start(bf16[80,384]{1,0:T(8,128)(2,1)S(1)} %bitcast.161), channel_id=1, source_target_pairs={{4,0},{8,4},{12,8},{5,1},{9,5},{13,9},{6,2},{10,6},{14,10},{7,3},{... | collective-permute-start | bytes 184328 | tf_op jit(solution)/shard_map/ppermute | solution.py:36
  82.5 6.9 %collective-permute-start.12 = (bf16[80,384]{1,0:T(8,128)(2,1)S(1)}, bf16[80,384]{1,0:T(8,128)(2,1)S(1)}, u32[]{:S(2)}, u32[]{:S(2)}) collective-permute-start(bf16[80,384]{1,0:T(8,128)(2,1)S(1)} %bitcast.163), channel_id=1, source_target_pairs={{0,4},{4,8},{8,12},{1,5},{5,9},{9,13},{2,6},{6,10},{10,14},{3,7},{... | collective-permute-start | bytes 184328 | tf_op jit(solution)/shard_map/ppermute | solution.py:35
  94.0 13.8 %all-to-all-start.1 = ((f32[80,4,256]{2,0,1:T(8,128)}), f32[80,4,256]{2,0,1:T(8,128)S(1)}, u32[]{:S(2)}, u32[]{:S(2)}) async-start(f32[80,4,256]{2,0,1:T(8,128)} %broadcast_select_fusion.1), calls=%async_computation.1 | async-start | bytes 655360 | tf_op jit(solution)/shard_map/all_to_all | solution.py:183
  (23 other events, 34.5 us)
